TPU v7x, 512 devices: a whole 4x4x16 slice. The times are simulated.
512 devices in a mesh: req: 32 (over y, x, core), grp: 16 (over z).
Axes of the slice: x: 4, y: 4, z: 16, core: 2. Of those that a mesh axis runs over, the one named last changes fastest.
Arguments:
- normed_token_input: bfloat16 [256, 8192], P(None, 'req'), may hold values from -6 to 6
- key_value_weight: bfloat16 [8192, 2048], P('req', 'grp'), may hold values from -0.0625 to 0.0625
- adapter_down_weight: bfloat16 [8192, 128, 128], P('req', 'grp'), may hold values from -0.0625 to 0.0625
- adapter_up_weight: bfloat16 [128, 64, 2048], P(None, None, 'grp'), may hold values from -0.75 to 0.75
- adapter_index_rows: int32 [256, 1], replicated, may hold values from 0 to 127
- queries: bfloat16 [256, 8192], P('req')
- key_value_pages: bfloat16 [10240, 16, 2, 8, 128], P('req', 'grp')
- lengths: int32 [256], P('req'), may hold values from 0 to 511, as said below
- page_slot_table: int32 [256, 32], P('req'), may hold values from 0 to 255, as said below
- departing_slots: int32 [1024], P('req'), may hold values from 0 to 255, as said below
- departing_target: int32 [1024, 1], P('req'), may hold values from 0 to 31; in each aligned block of 32 rows (0 to 31, 32 to 63, ...) at most 2 rows name the same one
Outputs:
- attention: bfloat16 [256, 8192], P('req')
- migrated_pool: bfloat16 [10240, 16, 2, 8, 128], P('req', 'grp')
Inputs may be any that keep to these rules, and one draw needn't show every extreme that they name: `adapter_index_rows`: each row names one adapter; every adapter is named by some request. `lengths`: some request has an empty cache and some has 511 cached tokens. `page_slot_table`: the rows of the requests of one home together name each of that home's slots 0 .. 255 exactly once. `departing_slots`: the 32 entries of one home are distinct. `departing_target`: the 32 rows of one home name one target at most 2 times; some home names some target exactly 2 times.
All inputs are finite; a program needn't handle non-finite values.
Results may differ from a plain program's by a relative error of at most 0.01345.
Values may be sent and summed in bfloat16 or wider, within the bound.
No kernel may reach another device: no remote copies, remote signals or barrier semaphores. Data moves between devices by JAX's collectives and lax.ppermute only.
A program may use at most 64 MiB of HBM per device.

v0:
```python
import math
import jax
import jax.numpy as jnp
from jax import lax
from jax.sharding import PartitionSpec as P

adapter_scale = 2.0
masked_score = -1e30


def shards(
    normed_token_input,
    key_value_weight,
    adapter_down_weight,
    adapter_up_weight,
    adapter_index_rows,
    queries,
    key_value_pages,
    lengths,
    page_slot_table,
    departing_slots,
    departing_target,
):
    selected_adapter = adapter_index_rows[:, 0]
    homes = lax.axis_size("req")
    groups = lax.axis_size("grp")
    home_index = lax.axis_index("req")
    group_index = lax.axis_index("grp")
    rows = lengths.shape[0]
    request_count = normed_token_input.shape[0]
    column_span = key_value_weight.shape[1]
    local_adapters = adapter_down_weight.shape[1]
    rank_width = adapter_down_weight.shape[2]
    rank_half = adapter_up_weight.shape[1]
    slot_tokens = key_value_pages.shape[1]
    heads = key_value_pages.shape[3]
    head_dim = key_value_pages.shape[4]
    key_width = heads * head_dim
    query_heads = queries.shape[1] // head_dim
    heads_per_target = query_heads // groups
    page_size = slot_tokens * groups
    pages = page_slot_table.shape[1]
    both = jnp.concatenate(
        [key_value_weight, adapter_down_weight.reshape(adapter_down_weight.shape[0], -1)], axis=1
    )
    products = jnp.dot(normed_token_input, both, preferred_element_type=jnp.float32)
    base_part = products[:, :column_span]
    down_all = products[:, column_span:].reshape(request_count, local_adapters, rank_width)
    local_choice = selected_adapter - group_index * local_adapters
    picker = (local_choice[:, None] == jnp.arange(local_adapters, dtype=jnp.int32)[None, :]).astype(
        jnp.float32
    )
    mid_part = jnp.einsum("ia,iaw->iw", picker, down_all)
    partial = jnp.concatenate([base_part, mid_part], axis=1).reshape(homes, rows, -1)
    summed = jnp.sum(lax.all_to_all(partial, "req", 0, 0, tiled=False), axis=0)
    base_resident = summed[:, :column_span]
    mid_owned = summed[:, column_span:].astype(jnp.bfloat16)
    resident_adapters = lax.dynamic_slice_in_dim(selected_adapter, home_index * rows, rows)
    owner = resident_adapters // local_adapters
    mid_spread = lax.all_to_all(
        jnp.broadcast_to(mid_owned[None], (groups,) + mid_owned.shape), "grp", 0, 0, tiled=False
    )
    request_index = jnp.arange(rows, dtype=jnp.int32)
    mid_home = mid_spread[owner, request_index]
    is_value = group_index * column_span >= key_width
    mid_used = jnp.where(is_value, mid_home[:, rank_half:], mid_home[:, :rank_half])
    up_weight_rows = adapter_up_weight[resident_adapters]
    adapter_update = jnp.einsum(
        "ir,irc->ic", mid_used, up_weight_rows, preferred_element_type=jnp.float32
    )
    fresh_columns = (base_resident + adapter_scale * adapter_update).astype(jnp.bfloat16)
    gathered = key_value_pages[page_slot_table][:, :, 0]
    keys = gathered[:, :, 0]
    values = gathered[:, :, 1]
    query = queries.reshape(rows, heads, -1, head_dim)
    scores = jnp.einsum(
        "ihgd,inhd->ihgn", query, keys, preferred_element_type=jnp.float32
    ) / math.sqrt(head_dim)
    positions = jnp.arange(pages, dtype=jnp.int32) * page_size + group_index * slot_tokens
    valid = (positions[None, :] < lengths[:, None])[:, None, None, :]
    scores = jnp.where(valid, scores, masked_score)
    local_top = jnp.max(scores, axis=3)
    weights = jnp.where(valid, jnp.exp(scores - local_top[..., None]), 0.0)
    local_total = jnp.sum(weights, axis=3)
    local_mixed = jnp.einsum("ihgn,inhd->ihgd", weights, values, preferred_element_type=jnp.float32)
    parcel = jnp.concatenate(
        [
            local_mixed.reshape(rows, groups, heads_per_target * head_dim),
            local_top.reshape(rows, groups, heads_per_target),
            local_total.reshape(rows, groups, heads_per_target),
            jnp.broadcast_to(
                fresh_columns.astype(jnp.float32)[:, None, :], (rows, groups, column_span)
            ),
        ],
        axis=2,
    ).transpose(1, 0, 2)
    received = lax.all_to_all(parcel, "grp", 0, 0, tiled=False)
    mixed_width = heads_per_target * head_dim
    shard_mixed = received[:, :, :mixed_width].reshape(groups, rows, heads_per_target, head_dim)
    shard_top = received[:, :, mixed_width : mixed_width + heads_per_target]
    shard_total = received[
        :, :, mixed_width + heads_per_target : mixed_width + 2 * heads_per_target
    ]
    new_all = received[:, :, mixed_width + 2 * heads_per_target :].astype(jnp.bfloat16)
    new_all = new_all.transpose(1, 0, 2).reshape(rows, groups * column_span)
    new_keys = new_all[:, :key_width].reshape(rows, heads, head_dim)
    new_values = new_all[:, key_width:].reshape(rows, heads, head_dim)
    head_of_target = group_index * heads_per_target // (query_heads // heads)
    own_query = lax.dynamic_slice_in_dim(
        queries, group_index * mixed_width, mixed_width, axis=1
    ).reshape(rows, heads_per_target, head_dim)
    own_key = lax.dynamic_index_in_dim(new_keys, head_of_target, 1, False)
    own_value = lax.dynamic_index_in_dim(new_values, head_of_target, 1, False)
    new_score = jnp.einsum(
        "ihd,id->ih", own_query, own_key, preferred_element_type=jnp.float32
    ) / math.sqrt(head_dim)
    top = jnp.maximum(jnp.max(shard_top, axis=0), new_score)
    shard_scale = jnp.exp(shard_top - top[None])
    new_weight = jnp.exp(new_score - top)
    total = jnp.sum(shard_total * shard_scale, axis=0) + new_weight
    mixed = (
        jnp.sum(shard_mixed * shard_scale[..., None], axis=0)
        + new_weight[..., None] * own_value.astype(jnp.float32)[:, None, :]
    )
    own_attention = (mixed / total[..., None]).astype(jnp.bfloat16).reshape(rows, mixed_width)
    attention = lax.all_gather(own_attention, "grp", axis=1, tiled=True)
    page_slot = page_slot_table[request_index, lengths // page_size]
    offset = lengths % page_size
    mine = offset // slot_tokens == group_index
    token_local = offset % slot_tokens
    current = key_value_pages[page_slot, token_local]
    fresh = jnp.stack([new_keys, new_values], axis=1)
    written = key_value_pages.at[page_slot, token_local].set(
        jnp.where(mine[:, None, None, None], fresh, current)
    )
    targets = departing_target[:, 0]
    count_out = departing_slots.shape[0]
    order = jnp.arange(count_out, dtype=jnp.int32)
    earlier = (targets[:, None] == targets[None, :]) & (order[None, :] < order[:, None])
    place = jnp.sum(earlier.astype(jnp.int32), axis=1)
    live_slots = rows * pages
    capacity = (key_value_pages.shape[0] - live_slots) // homes
    outbound = (
        jnp.zeros((homes, capacity) + key_value_pages.shape[1:], key_value_pages.dtype)
        .at[targets, place]
        .set(written[departing_slots])
    )
    arrived = lax.all_to_all(outbound, "req", split_axis=0, concat_axis=0, tiled=True)
    migrated_pool = jnp.concatenate(
        [written[:live_slots], arrived.reshape((homes * capacity,) + key_value_pages.shape[1:])],
        axis=0,
    )
    return (attention, migrated_pool)


def solution(mesh):
    in_specs = (
        P(None, "req"),
        P("req", "grp"),
        P("req", "grp", None),
        P(None, None, "grp"),
        P(),
        P("req", None),
        P("req", "grp", None, None, None),
        P("req"),
        P("req", None),
        P("req"),
        P("req", None),
    )
    out_specs = (P("req", None), P("req", "grp", None, None, None))
    return jax.shard_map(shards, mesh=mesh, in_specs=in_specs, out_specs=out_specs, check_vma=False)
```

profile of v0, /device:TPU:1, one launch (start us, length us, event | category | flops | bytes accessed | tf_op | source)
XLA Modules:
  0.0 158.4 jit_solution(13711185269570245694)
XLA Ops:
  0.7 1.5 copy.92
  5.8 1.3 multiply_reduce_fusion
  7.9 1.8 %copy.43 = f32[256,256]{1,0:T(8,128)} copy(f32[256,256]{0,1:T(8,128)} %pad_maximum_fusion.1) | data formatting | bytes 524288 | tf_op jit(solution)/shard_map/concatenate | solution.py:54
  9.7 11.0 %all-to-all-start = ((f32[32,8,256]{2,1,0:T(8,128)}), f32[32,8,256]{2,1,0:T(8,128)}, u32[]{:S(2)}, u32[]{:S(2)}) async-start(f32[32,8,256]{2,1,0:T(8,128)} %bitcast.113), calls=%async_computation | async-start | bytes 524288 | tf_op jit(solution)/shard_map/all_to_all | solution.py:55
  20.8 1.8 %gather_fusion = bf16[256,2,8,128]{3,2,1,0:T(8,128)(2,1)} fusion(bf16[320,2,8,128]{3,2,1,0:T(8,128)(2,1)S(1)} %bitcast.107, s32[1024]{0:T(1024)S(1)} %pad_clamp_fusion.2), kind=kCustom, calls=%fused_computation | custom fusion | bytes 2098176 | tf_op jit(solution)/shard_map/gather | solution.py:72
  22.6 2.1 %fusion.41 = (bf16[8,32,1,8,128]{4,3,2,1,0:T(8,128)(2,1)}, bf16[8,32,1,8,128]{4,3,2,1,0:T(8,128)(2,1)S(1)}) fusion(bf16[8,32,2,8,128]{4,3,2,1,0:T(8,128)(2,1)} %bitcast.110), kind=kLoop, calls=%fused_computation.114 | loop fusion | bytes 2097152 | tf_op jit(solution)/shard_map/slice | solution.py:74
  26.2 2.1 %fusion.5 = f32[8,8,8,128]{3,2,1,0:T(8,128)} fusion(bf16[8,32,1,8,128]{4,3,2,1,0:T(8,128)(2,1)} %get-tuple-element.6, f32[8,8,8,32]{3,2,1,0:T(8,128)} %copy-done.3, f32[8,8,8]{2,1,0:T(8,128)S(1)} %get-tuple-element.16, pred[8,32]{1,0:T(8,128)(4,1)S(1)} %broadcast_compare_fusion), kind=kOutput, calls=%fused_computation.20 | convolution fusion | flops 4227072 | bytes 854272 | tf_op jit(solution)/shard_map/ihgn,inhd->ihgd/dot_general | solution.py:85
  28.4 1.4 all-to-all-done
  31.4 12.5 %all-to-all-start.1 = ((bf16[16,8,128]{2,1,0:T(8,128)(2,1)}), bf16[16,8,128]{2,1,0:T(8,128)(2,1)}, u32[]{:S(2)}, u32[]{:S(2)}) async-start(bf16[16,8,128]{2,1,0:T(8,128)(2,1)} %broadcast_in_dim.45), calls=%async_computation.1 | async-start | bytes 65536 | tf_op jit(solution)/shard_map/all_to_all | solution.py:60
  46.4 1.7 %reshape.115 = f32[8,16,512]{2,1,0:T(8,128)} reshape(f32[8,8,8,128]{3,2,1,0:T(8,128)} %fusion.5) | data formatting | bytes 524288 | tf_op jit(solution)/shard_map/reshape | solution.py:88
  48.0 1.8 %copy.44 = f32[8,16,512]{2,0,1:T(8,128)} copy(f32[8,16,512]{2,1,0:T(8,128)} %reshape.115) | data formatting | bytes 524288 | tf_op jit(solution)/shard_map/reshape | solution.py:88
  49.8 1.2 pad_clamp_fusion.1
  51.1 1.3 gather_fusion.2
  52.4 3.1 %all-to-all-done.1 = bf16[16,8,128]{2,1,0:T(8,128)(2,1)} async-done(((bf16[16,8,128]{2,1,0:T(8,128)(2,1)}), bf16[16,8,128]{2,1,0:T(8,128)(2,1)}, u32[]{:S(2)}, u32[]{:S(2)}) %all-to-all-start.1) | async-done | bytes 32800 | tf_op jit(solution)/shard_map/all_to_all | solution.py:60
  55.5 1.9 %gather_fusion.1 = bf16[8,128]{1,0:T(8,128)(2,1)} fusion(bf16[16,8,128]{2,1,0:T(8,128)(2,1)} %all-to-all-done.1, s32[8]{0:T(128)S(1)} %get-tuple-element.12), kind=kCustom, calls=%fused_computation.1 | custom fusion | bytes 4160 | tf_op jit(solution)/shard_map/gather | solution.py:64
  59.3 1.8 %maximum_bitcast_fusion = f32[16,8,648]{2,1,0:T(8,128)} fusion(f32[8,16,128]{2,0,1:T(8,128)S(1)} %broadcast_in_dim.46, f32[8,16,4]{2,0,1:T(8,128)S(1)} %copy.46, f32[8,16,4]{2,0,1:T(8,128)S(1)} %copy.45, f32[8,16,512]{2,0,1:T(8,128)} %copy.44), kind=kLoop, calls=%fused_computation.22 | loop fusion | flops 248832 | bytes 663552 | tf_op jit(solution)/shard_map/transpose | solution.py:96
  61.1 8.4 %all-to-all-start.2 = ((f32[16,8,648]{2,1,0:T(8,128)}), f32[16,8,648]{2,1,0:T(8,128)}, u32[]{:S(2)}, u32[]{:S(2)}) async-start(f32[16,8,648]{2,1,0:T(8,128)} %maximum_bitcast_fusion), calls=%async_computation.2 | async-start | bytes 786432 | tf_op jit(solution)/shard_map/all_to_all | solution.py:97
  74.9 1.2 fusion.26
  76.7 10.9 %all-to-all-done.2 = f32[16,8,648]{2,1,0:T(8,128)} async-done(((f32[16,8,648]{2,1,0:T(8,128)}), f32[16,8,648]{2,1,0:T(8,128)}, u32[]{:S(2)}, u32[]{:S(2)}) %all-to-all-start.2) | async-done | bytes 331808 | tf_op jit(solution)/shard_map/all_to_all | solution.py:97
  93.5 28.5 %all_gather.3 = bf16[8,8192]{1,0:T(8,128)(2,1)} all-gather(bf16[8,512]{1,0:T(8,128)(2,1)S(1)} %fusion.15), channel_id=1, replica_groups=mesh['req'=32,'grp'=16] {'grp'}, dimensions={1}, use_global_device_ids=true | all-gather | bytes 139264 | tf_op jit(solution)/shard_map/all_gather | solution.py:126
  125.7 3.8 %scatter_fusion.1 = bf16[32,2,2,8,128]{4,3,2,1,0:T(8,128)(2,1)} fusion(bf16[32,2,2,8,128]{4,3,2,1,0:T(8,128)(2,1)} %broadcast.228, s32[32]{0:T(128)S(1)} %fusion.36, bf16[32,2,8,128]{3,2,1,0:T(8,128)(2,1)S(1)} %gather_fusion.5), kind=kCustom, calls=%fused_computation.7 | custom fusion | bytes 393472 | tf_op jit(solution)/shard_map/scatter | solution.py:146
  129.5 16.8 %all-to-all-start.3 = ((bf16[32,2,1,2,8,128]{5,4,3,1,2,0:T(8,128)(2,1)}), bf16[32,2,1,2,8,128]{5,4,3,1,2,0:T(8,128)(2,1)}, u32[]{:S(2)}, u32[]{:S(2)}) async-start(bf16[32,2,1,2,8,128]{5,4,3,1,2,0:T(8,128)(2,1)} %bitcast.112), calls=%async_computation.3 | async-start | bytes 524288 | tf_op jit(solution)/shard_map/all_to_all | solution.py:148
  147.4 7.8 %all-to-all-done.3 = bf16[32,2,1,2,8,128]{5,4,3,1,2,0:T(8,128)(2,1)} async-done(((bf16[32,2,1,2,8,128]{5,4,3,1,2,0:T(8,128)(2,1)}), bf16[32,2,1,2,8,128]{5,4,3,1,2,0:T(8,128)(2,1)}, u32[]{:S(2)}, u32[]{:S(2)}) %all-to-all-start.3) | async-done | bytes 262176 | tf_op jit(solution)/shard_map/all_to_all | solution.py:148
  155.2 2.5 %pad_maximum_fusion = bf16[320,1,2,8,128]{4,3,2,1,0:T(8,128)(2,1)} fusion(bf16[64,1,2,8,128]{4,3,2,1,0:T(8,128)(2,1)} %bitcast.43, bf16[256,1,2,8,128]{4,3,2,1,0:T(8,128)(2,1)} %slice_bitcast_fusion), kind=kLoop, calls=%fused_computation.9 | loop fusion | flops 655360 | bytes 2621440 | tf_op jit(solution)/shard_map/concatenate | solution.py:149
  (82 shorter events, 29.3 us)
Async XLA Ops:
  0.6 50.4 %copy-start = (bf16[128,64,128]{2,1,0:T(8,128)(2,1)S(1)}, bf16[128,64,128]{2,1,0:T(8,128)(2,1)}, u32[]{:S(2)}) copy-start(bf16[128,64,128]{2,1,0:T(8,128)(2,1)} %param.14) | copy-start | bytes 6291460
  0.6 1.7 %copy-start.6 = (bf16[256,256]{1,0:T(8,128)(2,1)S(1)}, bf16[256,256]{1,0:T(8,128)(2,1)}, u32[]{:S(2)}) copy-start(bf16[256,256]{1,0:T(8,128)(2,1)} %param.11) | copy-start | bytes 393220
  0.7 1.7 %copy-start.7 = (bf16[256,128]{1,0:T(8,128)(2,1)S(1)}, bf16[256,128]{1,0:T(8,128)(2,1)}, u32[]{:S(2)}) copy-start(bf16[256,128]{1,0:T(8,128)(2,1)} %param.12) | copy-start | bytes 196612
  0.7 1.6 %copy-start.4 = (bf16[256,8,128]{2,1,0:T(8,128)(2,1)S(1)}, bf16[256,8,128]{2,1,0:T(8,128)(2,1)}, u32[]{:S(2)}) copy-start(bf16[256,8,128]{2,1,0:T(8,128)(2,1)} %param.13) | copy-start | bytes 1572868
  2.7 1.4 copy-start.2
  2.8 1.4 copy-start.8
  4.1 3.1 %slice-start = ((f32[256,1152]{0,1:T(8,128)}), f32[256,128]{0,1:T(8,128)S(1)}, s32[]{:S(2)}) async-start(f32[256,1152]{0,1:T(8,128)} %copy-done.2), calls=%async_computation.4 | async-start | bytes 262144 | tf_op jit(solution)/shard_map/slice | solution.py:47
  5.8 14.9 %copy-start.1 = (s32[8,32]{1,0:T(8,128)S(1)}, s32[8,32]{1,0:T(8,128)}, u32[]{:S(2)}) copy-start(s32[8,32]{1,0:T(8,128)} %param.19) | copy-start | bytes 3076
  9.7 20.1 %all-to-all-start = ((f32[32,8,256]{2,1,0:T(8,128)}), f32[32,8,256]{2,1,0:T(8,128)}, u32[]{:S(2)}, u32[]{:S(2)}) async-start(f32[32,8,256]{2,1,0:T(8,128)} %bitcast.113), calls=%async_computation | async-start | bytes 524288 | tf_op jit(solution)/shard_map/all_to_all | solution.py:55
  22.6 2.1 %copy-start.11 = (s32[8]{0:T(128)S(1)}, s32[8]{0:T(128)}, u32[]{:S(2)}) copy-start(s32[8]{0:T(128)} %param.18) | copy-start | bytes 100
  22.6 2.2 %copy-start.10 = (bf16[8,8192]{1,0:T(8,128)(2,1)S(1)}, bf16[8,8192]{1,0:T(8,128)(2,1)}, u32[]{:S(2)}) copy-start(bf16[8,8192]{1,0:T(8,128)(2,1)} %param.16) | copy-start | bytes 393220
  24.8 19.1 %copy-start.9 = (s32[256,1]{0,1:T(1,128)S(1)}, s32[256,1]{0,1:T(1,128)}, u32[]{:S(2)}) copy-start(s32[256,1]{0,1:T(1,128)} %param.15) | copy-start | bytes 3076
  25.3 0.7 copy-start.3
  31.4 24.1 %all-to-all-start.1 = ((bf16[16,8,128]{2,1,0:T(8,128)(2,1)}), bf16[16,8,128]{2,1,0:T(8,128)(2,1)}, u32[]{:S(2)}, u32[]{:S(2)}) async-start(bf16[16,8,128]{2,1,0:T(8,128)(2,1)} %broadcast_in_dim.45), calls=%async_computation.1 | async-start | bytes 65536 | tf_op jit(solution)/shard_map/all_to_all | solution.py:60
  61.1 26.6 %all-to-all-start.2 = ((f32[16,8,648]{2,1,0:T(8,128)}), f32[16,8,648]{2,1,0:T(8,128)}, u32[]{:S(2)}, u32[]{:S(2)}) async-start(f32[16,8,648]{2,1,0:T(8,128)} %maximum_bitcast_fusion), calls=%async_computation.2 | async-start | bytes 786432 | tf_op jit(solution)/shard_map/all_to_all | solution.py:97
  129.5 25.7 %all-to-all-start.3 = ((bf16[32,2,1,2,8,128]{5,4,3,1,2,0:T(8,128)(2,1)}), bf16[32,2,1,2,8,128]{5,4,3,1,2,0:T(8,128)(2,1)}, u32[]{:S(2)}, u32[]{:S(2)}) async-start(bf16[32,2,1,2,8,128]{5,4,3,1,2,0:T(8,128)(2,1)} %bitcast.112), calls=%async_computation.3 | async-start | bytes 524288 | tf_op jit(solution)/shard_map/all_to_all | solution.py:148
  155.2 2.5 %copy-start.5 = (bf16[8,8192]{1,0:T(8,128)(2,1)S(1)}, bf16[8,8192]{1,0:T(8,128)(2,1)}, u32[]{:S(2)}) copy-start(bf16[8,8192]{1,0:T(8,128)(2,1)} %all_gather.3) | copy-start | bytes 393220
where the time goes:
time: 160 us; the launch traced here: 158 us
  starting transfers between devices  48.7 us (30%)
  local copies, waits for them, and re-layouts  32.1 us (20%)
  blocking collectives  28.5 us (18%)
  waiting for transfers between devices  23.2 us (14%)
  other arithmetic  20.9 us (13%)
  matrix products  4.13 us (3%)
    all_gather x1, blocking collectives, shards(): attention = lax.all_gather(own_attention, 'grp', axis=1, tiled=True)  28.5 us
    all_to_all x1, starting transfers between devices, shards(): lax.all_to_all(outbound, 'req', split_axis=0, concat_axis=0, tiled=True)  16.8 us
    all_to_all x1, starting transfers between devices, shards(): lax.all_to_all(jnp.broadcast_to(mid_owned[None], (groups,) + mid_owned.sh...  12.5 us
    all_to_all x1, starting transfers between devices, shards(): summed = jnp.sum(lax.all_to_all(partial, 'req', 0, 0, tiled=False), axis=0)  11 us
    all_to_all x1, waiting for transfers between devices, shards(): received = lax.all_to_all(parcel, 'grp', 0, 0, tiled=False)  10.9 us
    all_to_all x1, starting transfers between devices, shards(): received = lax.all_to_all(parcel, 'grp', 0, 0, tiled=False)  8.38 us
    all_to_all x1, waiting for transfers between devices, shards(): lax.all_to_all(outbound, 'req', split_axis=0, concat_axis=0, tiled=True)  7.77 us
    unnamed x29, local copies, waits for them, and re-layouts  4.87 us
  transfers between devices with their start and end apart: 4, of which 4 were waited for; matrix products, arithmetic and copies ran while one was open for 15% of the time, Pallas kernels for 0%

commit v1 on v0

--- a/solution.py
+++ b/solution.py
@@ -1,3 +1,4 @@
+import functools
 import math
 import jax
 import jax.numpy as jnp
@@ -6,6 +7,19 @@
 
 adapter_scale = 2.0
 masked_score = -1e30
+
+
+def _balance_quarters(original, axis_tag):
+    k_now = jnp.concatenate(
+        lax.all_to_all(
+            jnp.stack([original for _ in range(lax.axis_size(axis_tag))]), axis_tag, 0, 0
+        ),
+        axis=1,
+    )
+    return k_now
+
+
+tables_use = functools.partial(_balance_quarters, axis_tag="grp")
 
 
 def shards(
@@ -123,7 +137,7 @@
         + new_weight[..., None] * own_value.astype(jnp.float32)[:, None, :]
     )
     own_attention = (mixed / total[..., None]).astype(jnp.bfloat16).reshape(rows, mixed_width)
-    attention = lax.all_gather(own_attention, "grp", axis=1, tiled=True)
+    attention = tables_use(own_attention)
     page_slot = page_slot_table[request_index, lengths // page_size]
     offset = lengths % page_size
     mine = offset // slot_tokens == group_index

time: 160 us -> 143 us (0.89)
  blocking collectives: 28.5 us -> 0 us
  waiting for transfers between devices: 23.2 us -> 32 us
    all_gather x1 -> x0, blocking collectives: 28.5 us -> none  [shards(): attention = lax.all_gather(own_attention, 'grp', axis=1, tiled=True)]
    all_to_all x0 -> x1, waiting for transfers between devices: none -> 9.8 us  [_balance_quarters(): lax.all_to_all(jnp.stack([original for _ in range(lax.axis_size(axis_tag)...]
    all_to_all x0 -> x1, starting transfers between devices: none -> 6.05 us  [_balance_quarters(): lax.all_to_all(jnp.stack([original for _ in range(lax.axis_size(axis_tag)...]
    all_to_all x1, starting transfers between devices: 16.8 us -> 12.1 us  [shards(): lax.all_to_all(outbound, 'req', split_axis=0, concat_axis=0, tiled=True)]
    unnamed x29 -> x31, local copies, waits for them, and re-layouts: 4.87 us -> 4.86 us
  transfers between devices with their start and end apart: 4 -> 5, of which waited for: 4 -> 5; matrix products, arithmetic and copies ran while one was open for 15% -> 19% of each run, Pallas kernels for 0% -> 0%
where the time goes in v1:
time: 143 us; the launch traced here: 140 us
  starting transfers between devices  50.1 us (35%)
  waiting for transfers between devices  32 us (22%)
  local copies, waits for them, and re-layouts  31.7 us (22%)
  other arithmetic  21.3 us (15%)
  matrix products  4.13 us (3%)
    all_to_all x1, starting transfers between devices, shards(): lax.all_to_all(jnp.broadcast_to(mid_owned[None], (groups,) + mid_owned.sh...  12.5 us
    all_to_all x1, starting transfers between devices, shards(): lax.all_to_all(outbound, 'req', split_axis=0, concat_axis=0, tiled=True)  12.1 us
    all_to_all x1, starting transfers between devices, shards(): summed = jnp.sum(lax.all_to_all(partial, 'req', 0, 0, tiled=False), axis=0)  11 us
    all_to_all x1, waiting for transfers between devices, shards(): received = lax.all_to_all(parcel, 'grp', 0, 0, tiled=False)  10.9 us
    all_to_all x1, waiting for transfers between devices, _balance_quarters(): lax.all_to_all(jnp.stack([original for _ in range(lax.axis_size(axis_tag)...  9.8 us
    all_to_all x1, starting transfers between devices, shards(): received = lax.all_to_all(parcel, 'grp', 0, 0, tiled=False)  8.49 us
    all_to_all x1, waiting for transfers between devices, shards(): lax.all_to_all(outbound, 'req', split_axis=0, concat_axis=0, tiled=True)  6.91 us
    all_to_all x1, starting transfers between devices, _balance_quarters(): lax.all_to_all(jnp.stack([original for _ in range(lax.axis_size(axis_tag)...  6.05 us
  transfers between devices with their start and end apart: 5, of which 5 were waited for; matrix products, arithmetic and copies ran while one was open for 19% of the time, Pallas kernels for 0%

profile of v1, /device:TPU:1, one launch (start us, length us, event | category | flops | bytes accessed | tf_op | source)
XLA Modules:
  0.0 140.1 jit_solution(6995970577039890552)
XLA Ops:
  0.7 1.5 %copy.92 = bf16[320,1,2,8,128]{4,3,2,1,0:T(8,128)(2,1)S(1)} copy(bf16[320,1,2,8,128]{4,3,2,1,0:T(8,128)(2,1)} %param.17) | data formatting | bytes 2621440
  5.8 1.3 multiply_reduce_fusion
  7.9 1.8 %copy.43 = f32[256,256]{1,0:T(8,128)} copy(f32[256,256]{0,1:T(8,128)} %pad_maximum_fusion.1) | data formatting | bytes 524288 | tf_op jit(solution)/shard_map/concatenate | solution.py:68
  9.7 11.0 %all-to-all-start = ((f32[32,8,256]{2,1,0:T(8,128)}), f32[32,8,256]{2,1,0:T(8,128)}, u32[]{:S(2)}, u32[]{:S(2)}) async-start(f32[32,8,256]{2,1,0:T(8,128)} %bitcast.116), calls=%async_computation | async-start | bytes 524288 | tf_op jit(solution)/shard_map/all_to_all | solution.py:69
  20.8 1.8 %gather_fusion = bf16[256,2,8,128]{3,2,1,0:T(8,128)(2,1)} fusion(bf16[320,2,8,128]{3,2,1,0:T(8,128)(2,1)S(1)} %bitcast.110, s32[1024]{0:T(1024)S(1)} %pad_clamp_fusion.2), kind=kCustom, calls=%fused_computation | custom fusion | bytes 2098176 | tf_op jit(solution)/shard_map/gather | solution.py:86
  22.6 2.1 %fusion.41 = (bf16[8,32,1,8,128]{4,3,2,1,0:T(8,128)(2,1)}, bf16[8,32,1,8,128]{4,3,2,1,0:T(8,128)(2,1)S(1)}) fusion(bf16[8,32,2,8,128]{4,3,2,1,0:T(8,128)(2,1)} %bitcast.113), kind=kLoop, calls=%fused_computation.114 | loop fusion | bytes 2097152 | tf_op jit(solution)/shard_map/slice | solution.py:88
  26.2 2.1 %fusion.5 = f32[8,8,8,128]{3,2,1,0:T(8,128)} fusion(bf16[8,32,1,8,128]{4,3,2,1,0:T(8,128)(2,1)} %get-tuple-element.6, f32[8,8,8,32]{3,2,1,0:T(8,128)} %copy-done.3, f32[8,8,8]{2,1,0:T(8,128)S(1)} %get-tuple-element.16, pred[8,32]{1,0:T(8,128)(4,1)S(1)} %broadcast_compare_fusion), kind=kOutput, calls=%fused_computation.20 | convolution fusion | flops 4227072 | bytes 854272 | tf_op jit(solution)/shard_map/ihgn,inhd->ihgd/dot_general | solution.py:99
  28.4 1.4 all-to-all-done
  31.3 12.5 %all-to-all-start.1 = ((bf16[16,8,128]{2,1,0:T(8,128)(2,1)}), bf16[16,8,128]{2,1,0:T(8,128)(2,1)}, u32[]{:S(2)}, u32[]{:S(2)}) async-start(bf16[16,8,128]{2,1,0:T(8,128)(2,1)} %broadcast_in_dim.45), calls=%async_computation.1 | async-start | bytes 65536 | tf_op jit(solution)/shard_map/all_to_all | solution.py:74
  46.4 1.7 %reshape.125 = f32[8,16,512]{2,1,0:T(8,128)} reshape(f32[8,8,8,128]{3,2,1,0:T(8,128)} %fusion.5) | data formatting | bytes 524288 | tf_op jit(solution)/shard_map/reshape | solution.py:102
  48.1 1.8 %copy.44 = f32[8,16,512]{2,0,1:T(8,128)} copy(f32[8,16,512]{2,1,0:T(8,128)} %reshape.125) | data formatting | bytes 524288 | tf_op jit(solution)/shard_map/reshape | solution.py:102
  49.9 1.3 pad_clamp_fusion.1
  51.2 1.3 gather_fusion.2
  52.5 3.0 %all-to-all-done.1 = bf16[16,8,128]{2,1,0:T(8,128)(2,1)} async-done(((bf16[16,8,128]{2,1,0:T(8,128)(2,1)}), bf16[16,8,128]{2,1,0:T(8,128)(2,1)}, u32[]{:S(2)}, u32[]{:S(2)}) %all-to-all-start.1) | async-done | bytes 32800 | tf_op jit(solution)/shard_map/all_to_all | solution.py:74
  55.5 1.9 %gather_fusion.1 = bf16[8,128]{1,0:T(8,128)(2,1)} fusion(bf16[16,8,128]{2,1,0:T(8,128)(2,1)} %all-to-all-done.1, s32[8]{0:T(128)S(1)} %get-tuple-element.12), kind=kCustom, calls=%fused_computation.1 | custom fusion | bytes 4160 | tf_op jit(solution)/shard_map/gather | solution.py:78
  59.3 1.8 %maximum_bitcast_fusion = f32[16,8,648]{2,1,0:T(8,128)} fusion(f32[8,16,128]{2,0,1:T(8,128)S(1)} %broadcast_in_dim.46, f32[8,16,4]{2,0,1:T(8,128)S(1)} %copy.46, f32[8,16,4]{2,0,1:T(8,128)S(1)} %copy.45, f32[8,16,512]{2,0,1:T(8,128)} %copy.44), kind=kLoop, calls=%fused_computation.22 | loop fusion | flops 248832 | bytes 663552 | tf_op jit(solution)/shard_map/transpose | solution.py:110
  61.1 8.5 %all-to-all-start.2 = ((f32[16,8,648]{2,1,0:T(8,128)}), f32[16,8,648]{2,1,0:T(8,128)}, u32[]{:S(2)}, u32[]{:S(2)}) async-start(f32[16,8,648]{2,1,0:T(8,128)} %maximum_bitcast_fusion), calls=%async_computation.2 | async-start | bytes 786432 | tf_op jit(solution)/shard_map/all_to_all | solution.py:111
  76.9 10.9 %all-to-all-done.2 = f32[16,8,648]{2,1,0:T(8,128)} async-done(((f32[16,8,648]{2,1,0:T(8,128)}), f32[16,8,648]{2,1,0:T(8,128)}, u32[]{:S(2)}, u32[]{:S(2)}) %all-to-all-start.2) | async-done | bytes 331808 | tf_op jit(solution)/shard_map/all_to_all | solution.py:111
  95.8 3.8 %scatter_fusion.1 = bf16[32,2,2,8,128]{4,3,2,1,0:T(8,128)(2,1)} fusion(bf16[32,2,2,8,128]{4,3,2,1,0:T(8,128)(2,1)} %broadcast.232, s32[32]{0:T(128)S(1)} %fusion.36, bf16[32,2,8,128]{3,2,1,0:T(8,128)(2,1)S(1)} %gather_fusion.5), kind=kCustom, calls=%fused_computation.7 | custom fusion | bytes 393472 | tf_op jit(solution)/shard_map/scatter | solution.py:160
  99.6 12.1 %all-to-all-start.4 = ((bf16[32,2,1,2,8,128]{5,4,3,1,2,0:T(8,128)(2,1)}), bf16[32,2,1,2,8,128]{5,4,3,1,2,0:T(8,128)(2,1)}, u32[]{:S(2)}, u32[]{:S(2)}) async-start(bf16[32,2,1,2,8,128]{5,4,3,1,2,0:T(8,128)(2,1)} %bitcast.115), calls=%async_computation.4 | async-start | bytes 524288 | tf_op jit(solution)/shard_map/all_to_all | solution.py:162
  113.7 6.9 %all-to-all-done.4 = bf16[32,2,1,2,8,128]{5,4,3,1,2,0:T(8,128)(2,1)} async-done(((bf16[32,2,1,2,8,128]{5,4,3,1,2,0:T(8,128)(2,1)}), bf16[32,2,1,2,8,128]{5,4,3,1,2,0:T(8,128)(2,1)}, u32[]{:S(2)}, u32[]{:S(2)}) %all-to-all-start.4) | async-done | bytes 262176 | tf_op jit(solution)/shard_map/all_to_all | solution.py:162
  121.3 6.0 %all-to-all-start.3 = ((bf16[16,8,512]{2,1,0:T(8,128)(2,1)}), bf16[16,8,512]{2,1,0:T(8,128)(2,1)S(1)}, u32[]{:S(2)}, u32[]{:S(2)}) async-start(bf16[16,8,512]{2,1,0:T(8,128)(2,1)} %stack.6), calls=%async_computation.3 | async-start | bytes 262144 | tf_op jit(solution)/shard_map/all_to_all | solution.py:14
  127.5 2.1 %pad_maximum_fusion = bf16[320,1,2,8,128]{4,3,2,1,0:T(8,128)(2,1)} fusion(bf16[64,1,2,8,128]{4,3,2,1,0:T(8,128)(2,1)} %bitcast.45, bf16[256,1,2,8,128]{4,3,2,1,0:T(8,128)(2,1)S(1)} %slice_bitcast_fusion), kind=kLoop, calls=%fused_computation.9 | loop fusion | flops 655360 | bytes 2621440 | tf_op jit(solution)/shard_map/concatenate | solution.py:163
  129.6 9.8 %all-to-all-done.3 = bf16[16,8,512]{2,1,0:T(8,128)(2,1)S(1)} async-done(((bf16[16,8,512]{2,1,0:T(8,128)(2,1)}), bf16[16,8,512]{2,1,0:T(8,128)(2,1)S(1)}, u32[]{:S(2)}, u32[]{:S(2)}) %all-to-all-start.3) | async-done | bytes 131104 | tf_op jit(solution)/shard_map/all_to_all | solution.py:14
  (86 shorter events, 30.8 us)
Async XLA Ops:
  0.6 50.5 %copy-start = (bf16[128,64,128]{2,1,0:T(8,128)(2,1)S(1)}, bf16[128,64,128]{2,1,0:T(8,128)(2,1)}, u32[]{:S(2)}) copy-start(bf16[128,64,128]{2,1,0:T(8,128)(2,1)} %param.14) | copy-start | bytes 6291460
  0.6 1.7 %copy-start.5 = (bf16[256,256]{1,0:T(8,128)(2,1)S(1)}, bf16[256,256]{1,0:T(8,128)(2,1)}, u32[]{:S(2)}) copy-start(bf16[256,256]{1,0:T(8,128)(2,1)} %param.11) | copy-start | bytes 393220
  0.7 1.7 %copy-start.6 = (bf16[256,128]{1,0:T(8,128)(2,1)S(1)}, bf16[256,128]{1,0:T(8,128)(2,1)}, u32[]{:S(2)}) copy-start(bf16[256,128]{1,0:T(8,128)(2,1)} %param.12) | copy-start | bytes 196612
  0.7 1.6 %copy-start.4 = (bf16[256,8,128]{2,1,0:T(8,128)(2,1)S(1)}, bf16[256,8,128]{2,1,0:T(8,128)(2,1)}, u32[]{:S(2)}) copy-start(bf16[256,8,128]{2,1,0:T(8,128)(2,1)} %param.13) | copy-start | bytes 1572868
  2.7 1.4 copy-start.2
  2.8 1.4 copy-start.9
  4.1 3.1 %slice-start = ((f32[256,1152]{0,1:T(8,128)}), f32[256,128]{0,1:T(8,128)S(1)}, s32[]{:S(2)}) async-start(f32[256,1152]{0,1:T(8,128)} %copy-done.2), calls=%async_computation.5 | async-start | bytes 262144 | tf_op jit(solution)/shard_map/slice | solution.py:61
  5.8 14.9 %copy-start.1 = (s32[8,32]{1,0:T(8,128)S(1)}, s32[8,32]{1,0:T(8,128)}, u32[]{:S(2)}) copy-start(s32[8,32]{1,0:T(8,128)} %param.19) | copy-start | bytes 3076
  9.7 20.1 %all-to-all-start = ((f32[32,8,256]{2,1,0:T(8,128)}), f32[32,8,256]{2,1,0:T(8,128)}, u32[]{:S(2)}, u32[]{:S(2)}) async-start(f32[32,8,256]{2,1,0:T(8,128)} %bitcast.116), calls=%async_computation | async-start | bytes 524288 | tf_op jit(solution)/shard_map/all_to_all | solution.py:69
  22.6 2.1 %copy-start.12 = (s32[8]{0:T(128)S(1)}, s32[8]{0:T(128)}, u32[]{:S(2)}) copy-start(s32[8]{0:T(128)} %param.18) | copy-start | bytes 100
  22.6 2.2 %copy-start.11 = (bf16[8,8192]{1,0:T(8,128)(2,1)S(1)}, bf16[8,8192]{1,0:T(8,128)(2,1)}, u32[]{:S(2)}) copy-start(bf16[8,8192]{1,0:T(8,128)(2,1)} %param.16) | copy-start | bytes 393220
  24.8 19.1 %copy-start.10 = (s32[256,1]{0,1:T(1,128)S(1)}, s32[256,1]{0,1:T(1,128)}, u32[]{:S(2)}) copy-start(s32[256,1]{0,1:T(1,128)} %param.15) | copy-start | bytes 3076
  25.2 0.7 copy-start.3
  31.3 24.1 %all-to-all-start.1 = ((bf16[16,8,128]{2,1,0:T(8,128)(2,1)}), bf16[16,8,128]{2,1,0:T(8,128)(2,1)}, u32[]{:S(2)}, u32[]{:S(2)}) async-start(bf16[16,8,128]{2,1,0:T(8,128)(2,1)} %broadcast_in_dim.45), calls=%async_computation.1 | async-start | bytes 65536 | tf_op jit(solution)/shard_map/all_to_all | solution.py:74
  61.1 26.7 %all-to-all-start.2 = ((f32[16,8,648]{2,1,0:T(8,128)}), f32[16,8,648]{2,1,0:T(8,128)}, u32[]{:S(2)}, u32[]{:S(2)}) async-start(f32[16,8,648]{2,1,0:T(8,128)} %maximum_bitcast_fusion), calls=%async_computation.2 | async-start | bytes 786432 | tf_op jit(solution)/shard_map/all_to_all | solution.py:111
  92.8 20.7 %copy-start.8 = (f32[8,4]{1,0:T(8,128)S(1)}, f32[8,4]{1,0:T(8,128)}, u32[]{:S(2)}) copy-start(f32[8,4]{1,0:T(8,128)} %get-tuple-element.2) | copy-start | bytes 388
  92.8 20.8 %copy-start.7 = (f32[8,4]{1,0:T(8,128)S(1)}, f32[8,4]{1,0:T(8,128)}, u32[]{:S(2)}) copy-start(f32[8,4]{1,0:T(8,128)} %get-tuple-element.3) | copy-start | bytes 388
  99.6 21.0 %all-to-all-start.4 = ((bf16[32,2,1,2,8,128]{5,4,3,1,2,0:T(8,128)(2,1)}), bf16[32,2,1,2,8,128]{5,4,3,1,2,0:T(8,128)(2,1)}, u32[]{:S(2)}, u32[]{:S(2)}) async-start(bf16[32,2,1,2,8,128]{5,4,3,1,2,0:T(8,128)(2,1)} %bitcast.115), calls=%async_computation.4 | async-start | bytes 524288 | tf_op jit(solution)/shard_map/all_to_all | solution.py:162
  121.3 18.2 %all-to-all-start.3 = ((bf16[16,8,512]{2,1,0:T(8,128)(2,1)}), bf16[16,8,512]{2,1,0:T(8,128)(2,1)S(1)}, u32[]{:S(2)}, u32[]{:S(2)}) async-start(bf16[16,8,512]{2,1,0:T(8,128)(2,1)} %stack.6), calls=%async_computation.3 | async-start | bytes 262144 | tf_op jit(solution)/shard_map/all_to_all | solution.py:14
